TPU v7x, 512 devices: a whole 4x4x16 slice. The times are simulated.
512 devices in a mesh: seq: 32 (over z, core), tensor: 16 (over y, x).
Axes of the slice: x: 4, y: 4, z: 16, core: 2. Of those that a mesh axis runs over, the one named last changes fastest.
Arguments:
- hidden: bfloat16 [4, 64, 5120], P(None, None, 'seq'), may hold values from -400 to 400
- norm_gain: bfloat16 [5120], P('seq'), may hold values from 0.099609375 to 1.8984375
- w_qkv: bfloat16 [5120, 7168], P('seq', 'tensor'), may hold values from -0.078125 to 0.078125
- b_qkv: bfloat16 [7168], P('tensor'), may hold values from -3 to 3
- w_out: bfloat16 [5120, 5120], P('tensor', 'seq'), may hold values from -0.078125 to 0.078125
- prefix_key_cache: bfloat16 [16, 12288, 1024], P('tensor', 'seq'), may hold values from -140 to 140
- prefix_value_cache: bfloat16 [16, 12288, 1024], P('tensor', 'seq'), may hold values from -6 to 6
- suffix_key_cache: bfloat16 [64, 4096, 1024], P('tensor', 'seq'), may hold values from -8 to 8
- suffix_value_cache: bfloat16 [64, 4096, 1024], P('tensor', 'seq'), may hold values from -6 to 6
- prefix_lens: int32 [16], P('tensor'), may hold values from 1 to 12288, as said below
- suffix_lens: int32 [64], P('tensor'), may hold values from 0 to 4096, as said below
Outputs:
- attn_out: float32 [4, 64, 5120], P(None, 'tensor', 'seq')
- new_keys: float32 [64, 4, 1024], P('tensor')
- new_values: float32 [64, 4, 1024], P('tensor')
Inputs may be any that keep to these rules, and one draw needn't show every extreme that they name: `prefix_lens`: some group has exactly 12288 live slots and some exactly one. `suffix_lens`: some request has exactly 4096 live slots and some none.
All inputs are finite; a program needn't handle non-finite values.
Results may differ from a plain program's by a relative error of at most 0.012.
The roundings to bfloat16 on the way count: a program that leaves them out, or rounds other values in their place, can miss the bound.
Values may be sent and summed in bfloat16 or wider, within the bound.
No kernel may reach another device: no remote copies, remote signals or barrier semaphores. Data moves between devices by JAX's collectives and lax.ppermute only.
A program may use at most 64 MiB of HBM per device.

v0:
```python
import jax
import jax.numpy as jnp
from jax import lax
from jax.sharding import PartitionSpec as P

D = 5120
QUERY_HEADS = 40
KEY_HEADS = 8
HEAD_SIZE = 128
KEY_COLUMNS = 1024
SEQ = ("z", "core")
epsilon = 1e-06
masked_fill = -1e30


def apply_rotary(values, token_positions):
    half = values.shape[-1] // 2
    freq = jnp.exp(
        -(jnp.arange(half, dtype=jnp.float32) * (2.0 / values.shape[-1]))
        * jnp.log(jnp.float32(1000000.0))
    )
    angles = token_positions[..., None, None] * freq
    cosine = jnp.cos(angles)
    sine = jnp.sin(angles)
    left = values[..., :half]
    right = values[..., half:]
    return jnp.concatenate([left * cosine - right * sine, right * cosine + left * sine], axis=-1)


def body(
    hidden,
    norm_gain,
    w_qkv,
    b_qkv,
    w_out,
    prefix_key_cache,
    prefix_value_cache,
    suffix_key_cache,
    suffix_value_cache,
    prefix_lens,
    suffix_lens,
):
    seq_count = lax.axis_size(SEQ)
    tensor_count = lax.axis_size("tensor")
    steps = hidden.shape[0]
    request_total = hidden.shape[1]
    requests = suffix_lens.shape[0]
    columns = w_qkv.shape[1]
    prefix_count = prefix_key_cache.shape[1]
    suffix_count = suffix_key_cache.shape[1]
    query_group_width = QUERY_HEADS // KEY_HEADS
    query_width = QUERY_HEADS * HEAD_SIZE
    query_rows = steps * query_group_width
    scale = float(HEAD_SIZE) ** (-0.5)
    seq_index = lax.axis_index(SEQ)
    w_out_cols = lax.all_gather(w_out, "tensor", axis=0, tiled=True)
    xf = hidden.astype(jnp.float32)
    local_squares = jnp.sum(xf * xf, axis=2)
    squares = jnp.sum(
        lax.all_to_all(
            jnp.broadcast_to(local_squares[None], (seq_count,) + local_squares.shape),
            SEQ,
            0,
            0,
            tiled=True,
        ),
        axis=0,
    )
    normed = (
        xf * lax.rsqrt(squares / D + epsilon)[..., None] * norm_gain.astype(jnp.float32)
    ).astype(jnp.bfloat16)
    partial_value = jnp.einsum("sbd,dc->sbc", normed, w_qkv, preferred_element_type=jnp.float32)
    halves = seq_count // (steps * requests)
    half_width = columns // halves
    groups = request_total // requests
    core = lax.axis_index("core")
    plane_count = seq_count // halves
    by_half = partial_value.reshape(steps, groups, requests, halves, half_width)
    keep = lax.dynamic_index_in_dim(by_half, core, axis=3, keepdims=False)
    send = lax.dynamic_index_in_dim(by_half, 1 - core, axis=3, keepdims=False)
    pair_sum = keep + lax.ppermute(send, "core", [(0, 1), (1, 0)])
    chunks = pair_sum.transpose(0, 2, 1, 3).reshape(plane_count, groups, half_width)
    reduced = jnp.sum(lax.all_to_all(chunks, "z", 0, 0, tiled=True), axis=0)
    bias = lax.dynamic_slice_in_dim(
        b_qkv.astype(jnp.float32), seq_index % halves * half_width, half_width
    )
    reduced = reduced + bias[None, :]
    owned_rows = lax.all_to_all(reduced, "tensor", 0, 0, tiled=True)
    gathered = lax.all_gather(owned_rows, SEQ, axis=0, tiled=False)
    combined_output = (
        gathered.reshape(steps, requests, halves, tensor_count, half_width)
        .transpose(0, 1, 3, 2, 4)
        .reshape(steps, requests, tensor_count * columns)
    )
    token_positions = (
        (prefix_lens[0] + suffix_lens)[None, :] + jnp.arange(steps, dtype=jnp.int32)[:, None]
    ).astype(jnp.float32)
    query_matrix = apply_rotary(
        combined_output[..., :query_width].reshape(steps, requests, QUERY_HEADS, HEAD_SIZE),
        token_positions,
    ).astype(jnp.bfloat16)
    keys_float = apply_rotary(
        combined_output[..., query_width : query_width + KEY_COLUMNS].reshape(
            steps, requests, KEY_HEADS, HEAD_SIZE
        ),
        token_positions,
    )
    values_float = combined_output[..., query_width + KEY_COLUMNS :].reshape(
        steps, requests, KEY_HEADS, HEAD_SIZE
    )
    current_keys = keys_float.astype(jnp.bfloat16)
    current_values = values_float.astype(jnp.bfloat16)
    new_keys = keys_float.reshape(steps, requests, KEY_COLUMNS).transpose(1, 0, 2)
    new_values = values_float.reshape(steps, requests, KEY_COLUMNS).transpose(1, 0, 2)
    query_by_group = (
        query_matrix.reshape(steps, requests, KEY_HEADS, query_group_width, HEAD_SIZE)
        .transpose(1, 2, 0, 3, 4)
        .reshape(requests, KEY_HEADS, query_rows, HEAD_SIZE)
    )
    prefix_key_block = prefix_key_cache[0].reshape(prefix_count, KEY_HEADS, HEAD_SIZE)
    prefix_value_block = prefix_value_cache[0].reshape(prefix_count, KEY_HEADS, HEAD_SIZE)
    suffix_key_block = suffix_key_cache.reshape(requests, suffix_count, KEY_HEADS, HEAD_SIZE)
    suffix_value_block = suffix_value_cache.reshape(requests, suffix_count, KEY_HEADS, HEAD_SIZE)
    score_pre = (
        jnp.einsum(
            "rhqd,phd->rhqp", query_by_group, prefix_key_block, preferred_element_type=jnp.float32
        )
        * scale
    )
    score_suf = (
        jnp.einsum(
            "rhqd,rshd->rhqs", query_by_group, suffix_key_block, preferred_element_type=jnp.float32
        )
        * scale
    )
    pre_mask = (
        seq_index * prefix_count + jnp.arange(prefix_count, dtype=jnp.int32) < prefix_lens[0]
    )[None, None, None, :]
    suf_mask = (
        (seq_index * suffix_count + jnp.arange(suffix_count, dtype=jnp.int32))[None, :]
        < suffix_lens[:, None]
    )[:, None, None, :]
    fill_pre = jnp.where(pre_mask, score_pre, masked_fill)
    fill_suf = jnp.where(suf_mask, score_suf, masked_fill)
    local_max = jnp.maximum(jnp.max(fill_pre, axis=3), jnp.max(fill_suf, axis=3))
    prob_pre = jnp.where(pre_mask, jnp.exp(fill_pre - local_max[..., None]), 0.0)
    prob_suf = jnp.where(suf_mask, jnp.exp(fill_suf - local_max[..., None]), 0.0)
    local_weight = jnp.sum(prob_pre, axis=3) + jnp.sum(prob_suf, axis=3)
    local_acc = jnp.einsum(
        "rhqp,phd->rhqd",
        prob_pre.astype(jnp.bfloat16),
        prefix_value_block,
        preferred_element_type=jnp.float32,
    )
    local_acc = local_acc + jnp.einsum(
        "rhqs,rshd->rhqd",
        prob_suf.astype(jnp.bfloat16),
        suffix_value_block,
        preferred_element_type=jnp.float32,
    )
    fresh_k = current_keys.transpose(1, 2, 0, 3)
    fresh_v = current_values.transpose(1, 2, 0, 3)
    score_new = (
        jnp.einsum("rhqd,rhid->rhqi", query_by_group, fresh_k, preferred_element_type=jnp.float32)
        * scale
    )
    new_mask = (
        (jnp.arange(query_rows, dtype=jnp.int32) // query_group_width)[:, None]
        >= jnp.arange(steps, dtype=jnp.int32)[None, :]
    )[None, None]
    fill_new = jnp.where(new_mask, score_new, masked_fill)
    new_max = jnp.max(fill_new, axis=3)
    prob_new = jnp.where(new_mask, jnp.exp(fill_new - new_max[..., None]), 0.0)
    new_weight = jnp.sum(prob_new, axis=3)
    new_acc = jnp.einsum(
        "rhqi,rhid->rhqd",
        prob_new.astype(jnp.bfloat16),
        fresh_v,
        preferred_element_type=jnp.float32,
    )
    lane_pad = ((0, 0), (0, 0), (0, HEAD_SIZE - query_rows))
    packed = jnp.concatenate(
        [
            local_acc,
            jnp.pad(local_max, lane_pad)[:, :, None, :],
            jnp.pad(local_weight, lane_pad)[:, :, None, :],
        ],
        axis=2,
    ).reshape(requests, KEY_HEADS // 2, 2, query_rows + 2, HEAD_SIZE)
    keep = lax.dynamic_index_in_dim(packed, core, axis=2, keepdims=False)
    came = lax.ppermute(
        lax.dynamic_index_in_dim(packed, 1 - core, axis=2, keepdims=False), "core", [(0, 1), (1, 0)]
    )
    keep_max = keep[..., query_rows, :query_rows]
    came_max = came[..., query_rows, :query_rows]
    pair_max = jnp.maximum(keep_max, came_max)
    keep_factor = jnp.exp(keep_max - pair_max)
    came_factor = jnp.exp(came_max - pair_max)
    pair_weight = (
        keep[..., query_rows + 1, :query_rows] * keep_factor
        + came[..., query_rows + 1, :query_rows] * came_factor
    )
    pair_acc = (
        keep[..., :query_rows, :] * keep_factor[..., None]
        + came[..., :query_rows, :] * came_factor[..., None]
    )
    pad_rows = ((0, 0), (0, 0), (0, HEAD_SIZE - query_rows))
    pair_packed = jnp.concatenate(
        [
            pair_acc,
            jnp.pad(pair_max, pad_rows)[:, :, None, :],
            jnp.pad(pair_weight, pad_rows)[:, :, None, :],
        ],
        axis=2,
    ).reshape(seq_count // 2, query_rows + 2, HEAD_SIZE)
    arrived = lax.all_to_all(pair_packed, "z", 0, 0, tiled=True)
    w_out_cols, arrived = lax.optimization_barrier((w_out_cols, arrived))
    part_acc = arrived[:, :query_rows, :]
    part_max = arrived[:, query_rows, :query_rows]
    part_weight = arrived[:, query_rows + 1, :query_rows]
    global_max = jnp.max(part_max, axis=0)
    factor = jnp.exp(part_max - global_max[None])
    global_weight = jnp.sum(part_weight * factor, axis=0)
    global_acc = jnp.sum(part_acc * factor[..., None], axis=0)
    mine_r = seq_index // KEY_HEADS
    mine_h = seq_index % KEY_HEADS
    own_new_max = new_max[mine_r, mine_h]
    own_new_weight = new_weight[mine_r, mine_h]
    own_new_acc = new_acc[mine_r, mine_h]
    top = jnp.maximum(global_max, own_new_max)
    factor_old = jnp.exp(global_max - top)
    factor_new = jnp.exp(own_new_max - top)
    total = global_weight * factor_old + own_new_weight * factor_new
    summed = global_acc * factor_old[..., None] + own_new_acc * factor_new[..., None]
    attention_slice = (summed / total[..., None]).astype(jnp.bfloat16)
    attention_all = lax.all_to_all(
        jnp.broadcast_to(attention_slice[None], (seq_count,) + attention_slice.shape),
        SEQ,
        0,
        0,
        tiled=True,
    )
    heads_local = (
        attention_all.reshape(requests, KEY_HEADS, steps, query_group_width, HEAD_SIZE)
        .transpose(2, 0, 1, 3, 4)
        .reshape(steps, requests, query_width)
    )
    owned = jnp.einsum("sbc,cd->sbd", heads_local, w_out_cols, preferred_element_type=jnp.float32)
    return (owned, new_keys, new_values)


def solution(mesh):
    placed = (
        P(None, None, SEQ),
        P(SEQ),
        P(SEQ, "tensor"),
        P("tensor"),
        P("tensor", SEQ),
        P("tensor", SEQ, None),
        P("tensor", SEQ, None),
        P("tensor", SEQ, None),
        P("tensor", SEQ, None),
        P("tensor"),
        P("tensor"),
    )
    planes = jax.sharding.Mesh(
        mesh.devices.reshape(-1, 2, mesh.devices.shape[1]), ("z", "core", "tensor")
    )
    return jax.shard_map(
        body,
        mesh=planes,
        in_specs=placed,
        out_specs=(
            P(None, "tensor", ("z", "core")),
            P("tensor", None, None),
            P("tensor", None, None),
        ),
        check_vma=False,
    )
```

profile of v0, /device:TPU:1, one launch (start us, length us, event | category | flops | bytes accessed | tf_op | source)
XLA Modules:
  0.0 182.2 jit_solution(754688764741654744)
XLA Ops:
  7.2 1.1 fusion.20
  8.3 0.7 reshape.346
  9.0 16.7 %all-to-all-start = ((f32[32,1,256]{2,1,0:T(1,128)}), f32[32,1,256]{2,1,0:T(1,128)S(1)}, u32[]{:S(2)}, u32[]{:S(2)}) async-start(f32[32,1,256]{2,1,0:T(1,128)} %reshape.346), calls=%async_computation | async-start | bytes 65536 | tf_op jit(solution)/shard_map/all_to_all | solution.py:60
  25.8 0.7 all-gather.4.cloned.1.call-update
  26.5 0.7 convert_element_type.53
  27.2 10.7 %all-to-all-done = f32[32,1,256]{2,1,0:T(1,128)S(1)} async-done(((f32[32,1,256]{2,1,0:T(1,128)}), f32[32,1,256]{2,1,0:T(1,128)S(1)}, u32[]{:S(2)}, u32[]{:S(2)}) %all-to-all-start) | async-done | bytes 32800 | tf_op jit(solution)/shard_map/all_to_all | solution.py:60
  37.9 0.5 broadcast.183
  38.4 0.7 reduce.1
  39.3 1.2 fusion.28
  40.6 0.4 reshape.326
  41.0 0.5 constant_dynamic-slice_fusion.3
  41.6 3.2 %collective-permute-start = (f32[4,16,4,224]{3,1,2,0:T(8,128)S(1)}, f32[4,16,4,224]{3,1,2,0:T(8,128)S(1)}, u32[]{:S(2)}, u32[]{:S(2)}) collective-permute-start(f32[4,16,4,224]{3,1,2,0:T(8,128)S(1)} %bitcast.160), channel_id=1, source_target_pairs={{0,16},{16,0},{1,17},{17,1},{2,18},{18,2},{3,19},{19,3},{4,20},{20... | collective-permute-start | bytes 688136 | tf_op jit(solution)/shard_map/ppermute | solution.py:81
  45.5 0.4 collective-permute-done
  45.9 0.8 bitcast_add_fusion
  46.7 3.5 %all-to-all-start.1 = ((f32[16,16,224]{2,1,0:T(8,128)}), f32[16,16,224]{2,1,0:T(8,128)S(1)}, u32[]{:S(2)}, u32[]{:S(2)}) async-start(f32[16,16,224]{2,1,0:T(8,128)} %bitcast.6), calls=%async_computation.1 | async-start | bytes 524288 | tf_op jit(solution)/shard_map/all_to_all | solution.py:83
  50.5 14.1 %all-to-all-done.1 = f32[16,16,224]{2,1,0:T(8,128)S(1)} async-done(((f32[16,16,224]{2,1,0:T(8,128)}), f32[16,16,224]{2,1,0:T(8,128)S(1)}, u32[]{:S(2)}, u32[]{:S(2)}) %all-to-all-start.1) | async-done | bytes 229408 | tf_op jit(solution)/shard_map/all_to_all | solution.py:83
  64.6 0.6 reshape_add_fusion
  65.2 6.8 %all-to-all-start.2 = ((f32[16,1,224]{2,1,0:T(1,128)}), f32[16,1,224]{2,1,0:T(1,128)S(1)}, u32[]{:S(2)}, u32[]{:S(2)}) async-start(f32[16,1,224]{2,1,0:T(1,128)} %reshape_add_fusion), calls=%async_computation.2 | async-start | bytes 32768 | tf_op jit(solution)/shard_map/all_to_all | solution.py:88
  72.2 2.2 %copy.290 = bf16[48,8,8,128]{3,2,1,0:T(8,128)(2,1)} copy(bf16[48,8,8,128]{3,1,2,0:T(8,128)(2,1)} %bitcast.154) | data formatting | bytes 1572864
  74.4 4.0 %all-to-all-done.2 = f32[16,1,224]{2,1,0:T(1,128)S(1)} async-done(((f32[16,1,224]{2,1,0:T(1,128)}), f32[16,1,224]{2,1,0:T(1,128)S(1)}, u32[]{:S(2)}, u32[]{:S(2)}) %all-to-all-start.2) | async-done | bytes 14368 | tf_op jit(solution)/shard_map/all_to_all | solution.py:88
  78.4 38.2 %all-gather = f32[512,1,224]{2,0,1:T(8,128)S(1)} all-gather(f32[16,1,224]{2,0,1:T(8,128)S(1)} %copy.232), channel_id=2, replica_groups=mesh['z'=16,'core'=2,'tensor'=16] {'z','core'}, dimensions={0}, use_global_device_ids=true | all-gather | bytes 473088 | tf_op jit(solution)/shard_map/all_gather | solution.py:89
  116.7 0.4 copy.233
  117.1 0.8 reshape.329
  117.9 0.3 subtract_convert_fusion
  118.5 0.7 fusion.68
  119.1 0.7 fusion.69
  119.9 0.4 fusion.10
  120.4 0.5 convolution_bitcast_fusion
  120.9 0.3 fusion.18
  121.2 0.4 copy-done.2
  121.6 0.4 convolution_add_fusion
  122.3 2.1 %collective-permute-start.1 = (f32[4,4,22,128]{3,1,0,2:T(4,128)S(1)}, f32[4,4,22,128]{3,1,0,2:T(4,128)S(1)}, u32[]{:S(2)}, u32[]{:S(2)}) collective-permute-start(f32[4,4,22,128]{3,1,0,2:T(4,128)S(1)} %copy.256), channel_id=1, source_target_pairs={{0,16},{16,0},{1,17},{17,1},{2,18},{18,2},{3,19},{19,3},{4,20},{20... | collective-permute-start | bytes 540680 | tf_op jit(solution)/shard_map/ppermute | solution.py:191
  124.5 1.1 collective-permute-done.1
  125.9 0.2 fusion.27
  126.2 0.7 copy.259
  126.9 4.2 %all-to-all-start.3 = ((f32[16,22,128]{2,1,0:T(8,128)}), f32[16,22,128]{2,1,0:T(8,128)S(1)}, u32[]{:S(2)}, u32[]{:S(2)}) async-start(f32[16,22,128]{2,1,0:T(8,128)} %copy.259), calls=%async_computation.3 | async-start | bytes 393216 | tf_op jit(solution)/shard_map/all_to_all | solution.py:216
  131.3 0.3 fusion.67
  131.6 1.1 fusion.35
  132.8 2.2 %copy.228 = bf16[16,320,160]{1,0,2:T(8,128)(2,1)S(1)} copy(bf16[16,320,160]{1,2,0:T(8,128)(2,1)} %all-gather.4.cloned.1.call-done) | data formatting | bytes 3276800 | tf_op jit(solution)/shard_map/all_gather | solution.py:56
  135.0 2.5 %reshape.341 = bf16[5120,160]{0,1:T(8,128)(2,1)} reshape(bf16[16,320,160]{1,0,2:T(8,128)(2,1)S(1)} %copy.228) | data formatting | bytes 3276800 | tf_op jit(solution)/shard_map/optimization_barrier | solution.py:217
  137.5 6.8 %all-to-all-done.3 = f32[16,22,128]{2,1,0:T(8,128)S(1)} async-done(((f32[16,22,128]{2,1,0:T(8,128)}), f32[16,22,128]{2,1,0:T(8,128)S(1)}, u32[]{:S(2)}, u32[]{:S(2)}) %all-to-all-start.3) | async-done | bytes 180256 | tf_op jit(solution)/shard_map/all_to_all | solution.py:216
  144.6 0.9 fusion.46
  145.4 0.7 broadcast_in_dim.111
  146.2 9.2 %all-to-all-start.4 = ((bf16[32,20,128]{2,1,0:T(8,128)(2,1)}), bf16[32,20,128]{2,1,0:T(8,128)(2,1)S(1)}, u32[]{:S(2)}, u32[]{:S(2)}) async-start(bf16[32,20,128]{2,1,0:T(8,128)(2,1)} %broadcast_in_dim.111), calls=%async_computation.4 | async-start | bytes 393216 | tf_op jit(solution)/shard_map/all_to_all | solution.py:236
  155.3 0.7 copy.267
  156.0 0.7 fusion.47
  156.7 17.2 %all-to-all-done.4 = bf16[32,20,128]{2,1,0:T(8,128)(2,1)S(1)} async-done(((bf16[32,20,128]{2,1,0:T(8,128)(2,1)}), bf16[32,20,128]{2,1,0:T(8,128)(2,1)S(1)}, u32[]{:S(2)}, u32[]{:S(2)}) %all-to-all-start.4) | async-done | bytes 163872 | tf_op jit(solution)/shard_map/all_to_all | solution.py:236
  174.2 1.2 fusion
  (70 shorter events, 2.6 us)
Async XLA Ops:
  7.2 112.0 %copy-start = (bf16[4,128,1024]{2,1,0:T(8,128)(2,1)S(1)}, bf16[4,128,1024]{2,1,0:T(8,128)(2,1)}, u32[]{:S(2)}) copy-start(bf16[4,128,1024]{2,1,0:T(8,128)(2,1)} %param.18) | copy-start | bytes 3145732
  9.0 28.9 %all-to-all-start = ((f32[32,1,256]{2,1,0:T(1,128)}), f32[32,1,256]{2,1,0:T(1,128)S(1)}, u32[]{:S(2)}, u32[]{:S(2)}) async-start(f32[32,1,256]{2,1,0:T(1,128)} %reshape.346), calls=%async_computation | async-start | bytes 65536 | tf_op jit(solution)/shard_map/all_to_all | solution.py:60
  25.8 107.0 %all-gather.4.cloned.1.call-start = ((), (), s32[]{:S(2)}) async-start(), calls=%async_computation.5 | async-start | bytes 2088960 | tf_op jit(solution)/shard_map/all_gather | solution.py:56
  40.5 4.9 %copy-start.5 = (bf16[448]{0:T(512)(128)(2,1)S(1)}, bf16[448]{0:T(512)(128)(2,1)}, u32[]{:S(2)}) copy-start(bf16[448]{0:T(512)(128)(2,1)} %param.14) | copy-start | bytes 2692
  41.5 8.7 %copy-start.6 = (s32[4]{0:T(128)S(1)}, s32[4]{0:T(128)}, u32[]{:S(2)}) copy-start(s32[4]{0:T(128)} %param.21) | copy-start | bytes 52
  41.5 30.5 %copy-start.3 = (bf16[1,384,1024]{2,1,0:T(8,128)(2,1)S(1)}, bf16[1,384,1024]{2,1,0:T(8,128)(2,1)}, u32[]{:S(2)}) copy-start(bf16[1,384,1024]{2,1,0:T(8,128)(2,1)} %param.16) | copy-start | bytes 2359300
  41.6 4.3 %collective-permute-start = (f32[4,16,4,224]{3,1,2,0:T(8,128)S(1)}, f32[4,16,4,224]{3,1,2,0:T(8,128)S(1)}, u32[]{:S(2)}, u32[]{:S(2)}) collective-permute-start(f32[4,16,4,224]{3,1,2,0:T(8,128)S(1)} %bitcast.160), channel_id=1, source_target_pairs={{0,16},{16,0},{1,17},{17,1},{2,18},{18,2},{3,19},{19,3},{4,20},{20... | collective-permute-start | bytes 688136 | tf_op jit(solution)/shard_map/ppermute | solution.py:81
  46.7 17.9 %all-to-all-start.1 = ((f32[16,16,224]{2,1,0:T(8,128)}), f32[16,16,224]{2,1,0:T(8,128)S(1)}, u32[]{:S(2)}, u32[]{:S(2)}) async-start(f32[16,16,224]{2,1,0:T(8,128)} %bitcast.6), calls=%async_computation.1 | async-start | bytes 524288 | tf_op jit(solution)/shard_map/all_to_all | solution.py:83
  65.2 13.2 %all-to-all-start.2 = ((f32[16,1,224]{2,1,0:T(1,128)}), f32[16,1,224]{2,1,0:T(1,128)S(1)}, u32[]{:S(2)}, u32[]{:S(2)}) async-start(f32[16,1,224]{2,1,0:T(1,128)} %reshape_add_fusion), calls=%async_computation.2 | async-start | bytes 32768 | tf_op jit(solution)/shard_map/all_to_all | solution.py:88
  119.1 1.2 copy-start.4
  120.4 1.2 copy-start.2
  122.3 3.3 %collective-permute-start.1 = (f32[4,4,22,128]{3,1,0,2:T(4,128)S(1)}, f32[4,4,22,128]{3,1,0,2:T(4,128)S(1)}, u32[]{:S(2)}, u32[]{:S(2)}) collective-permute-start(f32[4,4,22,128]{3,1,0,2:T(4,128)S(1)} %copy.256), channel_id=1, source_target_pairs={{0,16},{16,0},{1,17},{17,1},{2,18},{18,2},{3,19},{19,3},{4,20},{20... | collective-permute-start | bytes 540680 | tf_op jit(solution)/shard_map/ppermute | solution.py:191
  126.9 17.4 %all-to-all-start.3 = ((f32[16,22,128]{2,1,0:T(8,128)}), f32[16,22,128]{2,1,0:T(8,128)S(1)}, u32[]{:S(2)}, u32[]{:S(2)}) async-start(f32[16,22,128]{2,1,0:T(8,128)} %copy.259), calls=%async_computation.3 | async-start | bytes 393216 | tf_op jit(solution)/shard_map/all_to_all | solution.py:216
  144.4 29.8 %copy-start.1 = (bf16[5120,160]{0,1:T(8,128)(2,1)S(1)}, bf16[5120,160]{0,1:T(8,128)(2,1)}, u32[]{:S(2)}) copy-start(bf16[5120,160]{0,1:T(8,128)(2,1)} %reshape.341) | copy-start | bytes 4915204
  146.2 27.8 %all-to-all-start.4 = ((bf16[32,20,128]{2,1,0:T(8,128)(2,1)}), bf16[32,20,128]{2,1,0:T(8,128)(2,1)S(1)}, u32[]{:S(2)}, u32[]{:S(2)}) async-start(bf16[32,20,128]{2,1,0:T(8,128)(2,1)} %broadcast_in_dim.111), calls=%async_computation.4 | async-start | bytes 393216 | tf_op jit(solution)/shard_map/all_to_all | solution.py:236
Sparse Core Ops, SparseCore 0:
  29.6 59.8 all-gather.3
where the time goes:
time: 183 us; the launch traced here: 182 us
  waiting for transfers between devices  54.9 us (30%)
  starting transfers between devices  45.7 us (25%)
  blocking collectives  38.2 us (21%)
  between operations  15.2 us (8%)
  local copies, waits for them, and re-layouts  14.3 us (8%)
  other arithmetic  7.77 us (4%)
  matrix products  6.08 us (3%)
    all_gather x1, blocking collectives, body(): gathered = lax.all_gather(owned_rows, SEQ, axis=0, tiled=False)  38.2 us
    all_to_all x1, waiting for transfers between devices, body(): lax.all_to_all(jnp.broadcast_to(attention_slice[None], (seq_count,) + att...  17.2 us
    all_to_all x1, starting transfers between devices, body(): lax.all_to_all(jnp.broadcast_to(local_squares[None], (seq_count,) + local...  16.7 us
    all_to_all x1, waiting for transfers between devices, body(): reduced = jnp.sum(lax.all_to_all(chunks, 'z', 0, 0, tiled=True), axis=0)  14.1 us
    all_to_all x1, waiting for transfers between devices, body(): lax.all_to_all(jnp.broadcast_to(local_squares[None], (seq_count,) + local...  10.7 us
    all_to_all x1, starting transfers between devices, body(): lax.all_to_all(jnp.broadcast_to(attention_slice[None], (seq_count,) + att...  9.18 us
    all_to_all x1, waiting for transfers between devices, body(): arrived = lax.all_to_all(pair_packed, 'z', 0, 0, tiled=True)  6.78 us
    all_to_all x1, starting transfers between devices, body(): owned_rows = lax.all_to_all(reduced, 'tensor', 0, 0, tiled=True)  6.76 us
  transfers between devices with their start and end apart: 8, of which 7 were waited for; matrix products, arithmetic and copies ran while one was open for 12% of the time, Pallas kernels for 0%

commit v1 on v0

--- a/solution.py
+++ b/solution.py
@@ -11,6 +11,29 @@
 SEQ = ("z", "core")
 epsilon = 1e-06
 masked_fill = -1e30
+
+
+def split_up(shard, dim, length):
+    dims = shard.shape
+    parts = shard.reshape(*dims[:dim], length, dims[dim] // length, *dims[dim + 1 :])
+    return jnp.moveaxis(parts, dim, 0)
+
+
+def joined_along(blocks, dim):
+    blocks = jnp.moveaxis(blocks, 0, dim)
+    shape = blocks.shape
+    return blocks.reshape(*shape[:dim], shape[dim] * shape[dim + 1], *shape[dim + 2 :])
+
+
+def swapped_with_each(x, axis, split_dim, concat_dim):
+    count, place = (lax.axis_size(axis), lax.axis_index(axis))
+    blocks = split_up(x, split_dim, count)
+    finished = [blocks[place]]
+    for turn in range(1, count):
+        sent = blocks[place ^ turn]
+        finished.append(lax.ppermute(sent, axis, [(i, i ^ turn) for i in range(count)]))
+    blocks = jnp.stack(finished)[place ^ jnp.arange(count)]
+    return joined_along(blocks, concat_dim)
 
 
 def apply_rotary(values, token_positions):
@@ -85,7 +108,7 @@
         b_qkv.astype(jnp.float32), seq_index % halves * half_width, half_width
     )
     reduced = reduced + bias[None, :]
-    owned_rows = lax.all_to_all(reduced, "tensor", 0, 0, tiled=True)
+    owned_rows = swapped_with_each(reduced, "tensor", 0, 0)
     gathered = lax.all_gather(owned_rows, SEQ, axis=0, tiled=False)
     combined_output = (
         gathered.reshape(steps, requests, halves, tensor_count, half_width)

time: 183 us -> 234 us (1.28)
  starting transfers between devices: 45.7 us -> 94.9 us
  waiting for transfers between devices: 54.9 us -> 51 us
  blocking collectives: 38.2 us -> 41.5 us
    ppermute x0 -> x15, starting transfers between devices: none -> 55.9 us  [swapped_with_each(): lax.ppermute(sent, axis, [(i, i ^ turn) for i in range(count)])]
    all_to_all x1 -> x0, starting transfers between devices: 6.76 us -> none  [body(): owned_rows = lax.all_to_all(reduced, 'tensor', 0, 0, tiled=True)]
    all_to_all x1 -> x0, waiting for transfers between devices: 3.98 us -> none  [body(): owned_rows = lax.all_to_all(reduced, 'tensor', 0, 0, tiled=True)]
    all_gather x1, blocking collectives: 38.2 us -> 41.5 us  [body(): gathered = lax.all_gather(owned_rows, SEQ, axis=0, tiled=False)]
  transfers between devices with their start and end apart: 8 -> 22, of which waited for: 7 -> 6; matrix products, arithmetic and copies ran while one was open for 12% -> 10% of each run, Pallas kernels for 0% -> 0%
where the time goes in v1:
time: 234 us; the launch traced here: 232 us
  starting transfers between devices  94.9 us (41%)
  waiting for transfers between devices  51 us (22%)
  blocking collectives  41.5 us (18%)
  local copies, waits for them, and re-layouts  15.9 us (7%)
  between operations  15.6 us (7%)
  other arithmetic  7.41 us (3%)
  matrix products  6.04 us (3%)
    ppermute x15, starting transfers between devices, swapped_with_each(): lax.ppermute(sent, axis, [(i, i ^ turn) for i in range(count)])  55.9 us
    all_gather x1, blocking collectives, body(): gathered = lax.all_gather(owned_rows, SEQ, axis=0, tiled=False)  41.5 us
    all_to_all x1, waiting for transfers between devices, body(): lax.all_to_all(jnp.broadcast_to(attention_slice[None], (seq_count,) + att...  17.9 us
    all_to_all x1, starting transfers between devices, body(): lax.all_to_all(jnp.broadcast_to(local_squares[None], (seq_count,) + local...  16.7 us
    all_to_all x1, waiting for transfers between devices, body(): reduced = jnp.sum(lax.all_to_all(chunks, 'z', 0, 0, tiled=True), axis=0)  14.1 us
    all_to_all x1, waiting for transfers between devices, body(): lax.all_to_all(jnp.broadcast_to(local_squares[None], (seq_count,) + local...  9.98 us
    all_to_all x1, starting transfers between devices, body(): lax.all_to_all(jnp.broadcast_to(attention_slice[None], (seq_count,) + att...  9.18 us
    all_to_all x1, waiting for transfers between devices, body(): arrived = lax.all_to_all(pair_packed, 'z', 0, 0, tiled=True)  6.82 us
  transfers between devices with their start and end apart: 22, of which 6 were waited for; matrix products, arithmetic and copies ran while one was open for 10% of the time, Pallas kernels for 0%

profile of v1, /device:TPU:1, one launch (start us, length us, event | category | flops | bytes accessed | tf_op | source)
XLA Modules:
  0.0 232.2 jit_solution(8645321821641879907)
XLA Ops:
  7.2 1.1 fusion.20
  8.3 0.7 reshape.377
  9.0 16.7 %all-to-all-start = ((f32[32,1,256]{2,1,0:T(1,128)}), f32[32,1,256]{2,1,0:T(1,128)S(1)}, u32[]{:S(2)}, u32[]{:S(2)}) async-start(f32[32,1,256]{2,1,0:T(1,128)} %reshape.377), calls=%async_computation | async-start | bytes 65536 | tf_op jit(solution)/shard_map/all_to_all | solution.py:83
  25.8 0.7 all-gather.4.cloned.1.call-update
  26.6 0.7 convert_element_type.53
  27.9 10.0 %all-to-all-done = f32[32,1,256]{2,1,0:T(1,128)S(1)} async-done(((f32[32,1,256]{2,1,0:T(1,128)}), f32[32,1,256]{2,1,0:T(1,128)S(1)}, u32[]{:S(2)}, u32[]{:S(2)}) %all-to-all-start) | async-done | bytes 32800 | tf_op jit(solution)/shard_map/all_to_all | solution.py:83
  38.4 0.7 reduce.1
  39.3 1.2 fusion.28
  41.6 3.2 %collective-permute-start = (f32[4,16,4,224]{3,1,2,0:T(8,128)S(1)}, f32[4,16,4,224]{3,1,2,0:T(8,128)S(1)}, u32[]{:S(2)}, u32[]{:S(2)}) collective-permute-start(f32[4,16,4,224]{3,1,2,0:T(8,128)S(1)} %bitcast.186), channel_id=1, source_target_pairs={{0,16},{16,0},{1,17},{17,1},{2,18},{18,2},{3,19},{19,3},{4,20},{20... | collective-permute-start | bytes 688136 | tf_op jit(solution)/shard_map/ppermute | solution.py:104
  45.0 0.9 collective-permute-done
  45.9 0.8 bitcast_add_fusion
  46.7 3.5 %all-to-all-start.1 = ((f32[16,16,224]{2,1,0:T(8,128)}), f32[16,16,224]{2,1,0:T(8,128)S(1)}, u32[]{:S(2)}, u32[]{:S(2)}) async-start(f32[16,16,224]{2,1,0:T(8,128)} %bitcast.6), calls=%async_computation.1 | async-start | bytes 524288 | tf_op jit(solution)/shard_map/all_to_all | solution.py:106
  50.5 14.1 %all-to-all-done.1 = f32[16,16,224]{2,1,0:T(8,128)S(1)} async-done(((f32[16,16,224]{2,1,0:T(8,128)}), f32[16,16,224]{2,1,0:T(8,128)S(1)}, u32[]{:S(2)}, u32[]{:S(2)}) %all-to-all-start.1) | async-done | bytes 229408 | tf_op jit(solution)/shard_map/all_to_all | solution.py:106
  64.7 4.4 %collective-permute-start.3 = (f32[1,224]{1,0:T(1,128)S(1)}, f32[1,224]{1,0:T(1,128)S(1)}, u32[]{:S(2)}, u32[]{:S(2)}) collective-permute-start(f32[1,224]{1,0:T(1,128)S(1)} %get-tuple-element.42), channel_id=1, source_target_pairs={{0,3},{1,2},{2,1},{3,0},{4,7},{5,6},{6,5},{7,4},{8,11},{9,10},{10,... | collective-permute-start | bytes 2696 | tf_op jit(solution)/shard_map/ppermute | solution.py:34
  69.1 3.2 %collective-permute-start.4 = (f32[1,224]{1,0:T(1,128)S(1)}, f32[1,224]{1,0:T(1,128)S(1)}, u32[]{:S(2)}, u32[]{:S(2)}) collective-permute-start(f32[1,224]{1,0:T(1,128)S(1)} %get-tuple-element.41), channel_id=1, source_target_pairs={{0,4},{1,5},{2,6},{3,7},{4,0},{5,1},{6,2},{7,3},{8,12},{9,13},{10,... | collective-permute-start | bytes 2696 | tf_op jit(solution)/shard_map/ppermute | solution.py:34
  72.4 1.9 collective-permute-start.5
  74.3 4.2 %collective-permute-start.6 = (f32[1,224]{1,0:T(1,128)S(1)}, f32[1,224]{1,0:T(1,128)S(1)}, u32[]{:S(2)}, u32[]{:S(2)}) collective-permute-start(f32[1,224]{1,0:T(1,128)S(1)} %get-tuple-element.39), channel_id=1, source_target_pairs={{0,6},{1,7},{2,4},{3,5},{4,2},{5,3},{6,0},{7,1},{8,14},{9,15},{10,... | collective-permute-start | bytes 2696 | tf_op jit(solution)/shard_map/ppermute | solution.py:34
  78.5 4.3 %collective-permute-start.7 = (f32[1,224]{1,0:T(1,128)S(1)}, f32[1,224]{1,0:T(1,128)S(1)}, u32[]{:S(2)}, u32[]{:S(2)}) collective-permute-start(f32[1,224]{1,0:T(1,128)S(1)} %get-tuple-element.38), channel_id=1, source_target_pairs={{0,7},{1,6},{2,5},{3,4},{4,3},{5,2},{6,1},{7,0},{8,15},{9,14},{10,... | collective-permute-start | bytes 2696 | tf_op jit(solution)/shard_map/ppermute | solution.py:34
  82.8 4.8 %collective-permute-start.8 = (f32[1,224]{1,0:T(1,128)S(1)}, f32[1,224]{1,0:T(1,128)S(1)}, u32[]{:S(2)}, u32[]{:S(2)}) collective-permute-start(f32[1,224]{1,0:T(1,128)S(1)} %get-tuple-element.37), channel_id=1, source_target_pairs={{0,8},{1,9},{2,10},{3,11},{4,12},{5,13},{6,14},{7,15},{8,0},{9,1},... | collective-permute-start | bytes 2696 | tf_op jit(solution)/shard_map/ppermute | solution.py:34
  87.6 1.9 collective-permute-start.9
  89.6 5.7 %collective-permute-start.10 = (f32[1,224]{1,0:T(1,128)S(1)}, f32[1,224]{1,0:T(1,128)S(1)}, u32[]{:S(2)}, u32[]{:S(2)}) collective-permute-start(f32[1,224]{1,0:T(1,128)S(1)} %get-tuple-element.35), channel_id=1, source_target_pairs={{0,10},{1,11},{2,8},{3,9},{4,14},{5,15},{6,12},{7,13},{8,2},{9,3},... | collective-permute-start | bytes 2696 | tf_op jit(solution)/shard_map/ppermute | solution.py:34
  95.3 4.2 %collective-permute-start.11 = (f32[1,224]{1,0:T(1,128)S(1)}, f32[1,224]{1,0:T(1,128)S(1)}, u32[]{:S(2)}, u32[]{:S(2)}) collective-permute-start(f32[1,224]{1,0:T(1,128)S(1)} %get-tuple-element.34), channel_id=1, source_target_pairs={{0,11},{1,10},{2,9},{3,8},{4,15},{5,14},{6,13},{7,12},{8,3},{9,2},... | collective-permute-start | bytes 2696 | tf_op jit(solution)/shard_map/ppermute | solution.py:34
  99.4 4.6 %collective-permute-start.12 = (f32[1,224]{1,0:T(1,128)S(1)}, f32[1,224]{1,0:T(1,128)S(1)}, u32[]{:S(2)}, u32[]{:S(2)}) collective-permute-start(f32[1,224]{1,0:T(1,128)S(1)} %get-tuple-element.33), channel_id=1, source_target_pairs={{0,12},{1,13},{2,14},{3,15},{4,8},{5,9},{6,10},{7,11},{8,4},{9,5},... | collective-permute-start | bytes 2696 | tf_op jit(solution)/shard_map/ppermute | solution.py:34
  104.1 1.9 collective-permute-start.13
  106.0 5.4 %collective-permute-start.14 = (f32[1,224]{1,0:T(1,128)S(1)}, f32[1,224]{1,0:T(1,128)S(1)}, u32[]{:S(2)}, u32[]{:S(2)}) collective-permute-start(f32[1,224]{1,0:T(1,128)S(1)} %get-tuple-element.31), channel_id=1, source_target_pairs={{0,14},{1,15},{2,12},{3,13},{4,10},{5,11},{6,8},{7,9},{8,6},{9,7},... | collective-permute-start | bytes 2696 | tf_op jit(solution)/shard_map/ppermute | solution.py:34
  111.4 4.1 %collective-permute-start.15 = (f32[1,224]{1,0:T(1,128)S(1)}, f32[1,224]{1,0:T(1,128)S(1)}, u32[]{:S(2)}, u32[]{:S(2)}) collective-permute-start(f32[1,224]{1,0:T(1,128)S(1)} %get-tuple-element.30), channel_id=1, source_target_pairs={{0,15},{1,14},{2,13},{3,12},{4,11},{5,10},{6,9},{7,8},{8,7},{9,6},... | collective-permute-start | bytes 2696 | tf_op jit(solution)/shard_map/ppermute | solution.py:34
  115.6 1.9 collective-permute-start.1
  117.5 3.4 %collective-permute-start.2 = (f32[1,224]{1,0:T(1,128)S(1)}, f32[1,224]{1,0:T(1,128)S(1)}, u32[]{:S(2)}, u32[]{:S(2)}) collective-permute-start(f32[1,224]{1,0:T(1,128)S(1)} %get-tuple-element.43), channel_id=1, source_target_pairs={{0,2},{1,3},{2,0},{3,1},{4,6},{5,7},{6,4},{7,5},{8,10},{9,11},{10,... | collective-permute-start | bytes 2696 | tf_op jit(solution)/shard_map/ppermute | solution.py:34
  121.1 2.2 copy.239
  124.0 41.5 %all-gather = f32[512,224]{1,0:T(8,128)S(1)} all-gather(f32[16,224]{1,0:T(8,128)S(1)} %gather_fusion), channel_id=2, replica_groups=mesh['z'=16,'core'=2,'tensor'=16] {'z','core'}, dimensions={0}, use_global_device_ids=true | all-gather | bytes 473088 | tf_op jit(solution)/shard_map/all_gather | solution.py:112
  165.9 0.8 reshape.350
  167.8 0.7 fusion.70
  168.5 0.7 fusion.71
  170.8 0.7 copy-done.2
  172.3 2.1 collective-permute-start.16
  174.4 0.6 slice_bitcast_fusion.1
  176.1 0.7 copy.212
  176.9 4.2 %all-to-all-start.2 = ((f32[16,22,128]{2,1,0:T(8,128)}), f32[16,22,128]{2,1,0:T(8,128)S(1)}, u32[]{:S(2)}, u32[]{:S(2)}) async-start(f32[16,22,128]{2,1,0:T(8,128)} %copy.212), calls=%async_computation.2 | async-start | bytes 393216 | tf_op jit(solution)/shard_map/all_to_all | solution.py:239
  181.6 1.1 fusion.35
  182.7 2.2 copy.182
  184.9 2.6 %reshape.372 = bf16[5120,160]{0,1:T(8,128)(2,1)} reshape(bf16[16,320,160]{1,0,2:T(8,128)(2,1)S(1)} %copy.182) | data formatting | bytes 3276800 | tf_op jit(solution)/shard_map/optimization_barrier | solution.py:240
  187.5 6.8 %all-to-all-done.2 = f32[16,22,128]{2,1,0:T(8,128)S(1)} async-done(((f32[16,22,128]{2,1,0:T(8,128)}), f32[16,22,128]{2,1,0:T(8,128)S(1)}, u32[]{:S(2)}, u32[]{:S(2)}) %all-to-all-start.2) | async-done | bytes 180256 | tf_op jit(solution)/shard_map/all_to_all | solution.py:239
  194.6 0.9 fusion.46
  195.5 0.7 broadcast_in_dim.112
  196.2 9.2 %all-to-all-start.3 = ((bf16[32,20,128]{2,1,0:T(8,128)(2,1)}), bf16[32,20,128]{2,1,0:T(8,128)(2,1)S(1)}, u32[]{:S(2)}, u32[]{:S(2)}) async-start(bf16[32,20,128]{2,1,0:T(8,128)(2,1)} %broadcast_in_dim.112), calls=%async_computation.3 | async-start | bytes 393216 | tf_op jit(solution)/shard_map/all_to_all | solution.py:259
  205.4 0.7 fusion.47
  206.1 17.9 %all-to-all-done.3 = bf16[32,20,128]{2,1,0:T(8,128)(2,1)S(1)} async-done(((bf16[32,20,128]{2,1,0:T(8,128)(2,1)}), bf16[32,20,128]{2,1,0:T(8,128)(2,1)S(1)}, u32[]{:S(2)}, u32[]{:S(2)}) %all-to-all-start.3) | async-done | bytes 163872 | tf_op jit(solution)/shard_map/all_to_all | solution.py:259
  224.2 1.2 fusion
  (99 shorter events, 8.8 us)
Async XLA Ops:
  7.2 161.3 %copy-start = (bf16[4,128,1024]{2,1,0:T(8,128)(2,1)S(1)}, bf16[4,128,1024]{2,1,0:T(8,128)(2,1)}, u32[]{:S(2)}) copy-start(bf16[4,128,1024]{2,1,0:T(8,128)(2,1)} %param.18) | copy-start | bytes 3145732
  9.0 28.9 %all-to-all-start = ((f32[32,1,256]{2,1,0:T(1,128)}), f32[32,1,256]{2,1,0:T(1,128)S(1)}, u32[]{:S(2)}, u32[]{:S(2)}) async-start(f32[32,1,256]{2,1,0:T(1,128)} %reshape.377), calls=%async_computation | async-start | bytes 65536 | tf_op jit(solution)/shard_map/all_to_all | solution.py:83
  25.8 156.9 %all-gather.4.cloned.1.call-start = ((), (), s32[]{:S(2)}) async-start(), calls=%async_computation.4 | async-start | bytes 2088960 | tf_op jit(solution)/shard_map/all_gather | solution.py:79
  40.5 4.3 %copy-start.5 = (bf16[448]{0:T(512)(128)(2,1)S(1)}, bf16[448]{0:T(512)(128)(2,1)}, u32[]{:S(2)}) copy-start(bf16[448]{0:T(512)(128)(2,1)} %param.14) | copy-start | bytes 2692
  41.5 8.7 %copy-start.6 = (s32[4]{0:T(128)S(1)}, s32[4]{0:T(128)}, u32[]{:S(2)}) copy-start(s32[4]{0:T(128)} %param.21) | copy-start | bytes 52
  41.5 79.4 %copy-start.3 = (bf16[1,384,1024]{2,1,0:T(8,128)(2,1)S(1)}, bf16[1,384,1024]{2,1,0:T(8,128)(2,1)}, u32[]{:S(2)}) copy-start(bf16[1,384,1024]{2,1,0:T(8,128)(2,1)} %param.16) | copy-start | bytes 2359300
  41.6 4.3 %collective-permute-start = (f32[4,16,4,224]{3,1,2,0:T(8,128)S(1)}, f32[4,16,4,224]{3,1,2,0:T(8,128)S(1)}, u32[]{:S(2)}, u32[]{:S(2)}) collective-permute-start(f32[4,16,4,224]{3,1,2,0:T(8,128)S(1)} %bitcast.186), channel_id=1, source_target_pairs={{0,16},{16,0},{1,17},{17,1},{2,18},{18,2},{3,19},{19,3},{4,20},{20... | collective-permute-start | bytes 688136 | tf_op jit(solution)/shard_map/ppermute | solution.py:104
  46.7 17.9 %all-to-all-start.1 = ((f32[16,16,224]{2,1,0:T(8,128)}), f32[16,16,224]{2,1,0:T(8,128)S(1)}, u32[]{:S(2)}, u32[]{:S(2)}) async-start(f32[16,16,224]{2,1,0:T(8,128)} %bitcast.6), calls=%async_computation.1 | async-start | bytes 524288 | tf_op jit(solution)/shard_map/all_to_all | solution.py:106
  64.7 18.0 %collective-permute-start.3 = (f32[1,224]{1,0:T(1,128)S(1)}, f32[1,224]{1,0:T(1,128)S(1)}, u32[]{:S(2)}, u32[]{:S(2)}) collective-permute-start(f32[1,224]{1,0:T(1,128)S(1)} %get-tuple-element.42), channel_id=1, source_target_pairs={{0,3},{1,2},{2,1},{3,0},{4,7},{5,6},{6,5},{7,4},{8,11},{9,10},{10,... | collective-permute-start | bytes 2696 | tf_op jit(solution)/shard_map/ppermute | solution.py:34
  69.1 18.5 %collective-permute-start.4 = (f32[1,224]{1,0:T(1,128)S(1)}, f32[1,224]{1,0:T(1,128)S(1)}, u32[]{:S(2)}, u32[]{:S(2)}) collective-permute-start(f32[1,224]{1,0:T(1,128)S(1)} %get-tuple-element.41), channel_id=1, source_target_pairs={{0,4},{1,5},{2,6},{3,7},{4,0},{5,1},{6,2},{7,3},{8,12},{9,13},{10,... | collective-permute-start | bytes 2696 | tf_op jit(solution)/shard_map/ppermute | solution.py:34
  72.4 17.2 %collective-permute-start.5 = (f32[1,224]{1,0:T(1,128)S(1)}, f32[1,224]{1,0:T(1,128)S(1)}, u32[]{:S(2)}, u32[]{:S(2)}) collective-permute-start(f32[1,224]{1,0:T(1,128)S(1)} %get-tuple-element.40), channel_id=1, source_target_pairs={{0,5},{1,4},{2,7},{3,6},{4,1},{5,0},{6,3},{7,2},{8,13},{9,12},{10,... | collective-permute-start | bytes 2696 | tf_op jit(solution)/shard_map/ppermute | solution.py:34
  74.3 21.0 %collective-permute-start.6 = (f32[1,224]{1,0:T(1,128)S(1)}, f32[1,224]{1,0:T(1,128)S(1)}, u32[]{:S(2)}, u32[]{:S(2)}) collective-permute-start(f32[1,224]{1,0:T(1,128)S(1)} %get-tuple-element.39), channel_id=1, source_target_pairs={{0,6},{1,7},{2,4},{3,5},{4,2},{5,3},{6,0},{7,1},{8,14},{9,15},{10,... | collective-permute-start | bytes 2696 | tf_op jit(solution)/shard_map/ppermute | solution.py:34
  78.5 21.0 %collective-permute-start.7 = (f32[1,224]{1,0:T(1,128)S(1)}, f32[1,224]{1,0:T(1,128)S(1)}, u32[]{:S(2)}, u32[]{:S(2)}) collective-permute-start(f32[1,224]{1,0:T(1,128)S(1)} %get-tuple-element.38), channel_id=1, source_target_pairs={{0,7},{1,6},{2,5},{3,4},{4,3},{5,2},{6,1},{7,0},{8,15},{9,14},{10,... | collective-permute-start | bytes 2696 | tf_op jit(solution)/shard_map/ppermute | solution.py:34
  82.8 21.3 %collective-permute-start.8 = (f32[1,224]{1,0:T(1,128)S(1)}, f32[1,224]{1,0:T(1,128)S(1)}, u32[]{:S(2)}, u32[]{:S(2)}) collective-permute-start(f32[1,224]{1,0:T(1,128)S(1)} %get-tuple-element.37), channel_id=1, source_target_pairs={{0,8},{1,9},{2,10},{3,11},{4,12},{5,13},{6,14},{7,15},{8,0},{9,1},... | collective-permute-start | bytes 2696 | tf_op jit(solution)/shard_map/ppermute | solution.py:34
  87.6 18.4 %collective-permute-start.9 = (f32[1,224]{1,0:T(1,128)S(1)}, f32[1,224]{1,0:T(1,128)S(1)}, u32[]{:S(2)}, u32[]{:S(2)}) collective-permute-start(f32[1,224]{1,0:T(1,128)S(1)} %get-tuple-element.36), channel_id=1, source_target_pairs={{0,9},{1,8},{2,11},{3,10},{4,13},{5,12},{6,15},{7,14},{8,1},{9,0},... | collective-permute-start | bytes 2696 | tf_op jit(solution)/shard_map/ppermute | solution.py:34
  89.6 21.9 %collective-permute-start.10 = (f32[1,224]{1,0:T(1,128)S(1)}, f32[1,224]{1,0:T(1,128)S(1)}, u32[]{:S(2)}, u32[]{:S(2)}) collective-permute-start(f32[1,224]{1,0:T(1,128)S(1)} %get-tuple-element.35), channel_id=1, source_target_pairs={{0,10},{1,11},{2,8},{3,9},{4,14},{5,15},{6,12},{7,13},{8,2},{9,3},... | collective-permute-start | bytes 2696 | tf_op jit(solution)/shard_map/ppermute | solution.py:34
  95.3 20.3 %collective-permute-start.11 = (f32[1,224]{1,0:T(1,128)S(1)}, f32[1,224]{1,0:T(1,128)S(1)}, u32[]{:S(2)}, u32[]{:S(2)}) collective-permute-start(f32[1,224]{1,0:T(1,128)S(1)} %get-tuple-element.34), channel_id=1, source_target_pairs={{0,11},{1,10},{2,9},{3,8},{4,15},{5,14},{6,13},{7,12},{8,3},{9,2},... | collective-permute-start | bytes 2696 | tf_op jit(solution)/shard_map/ppermute | solution.py:34
  99.4 18.1 %collective-permute-start.12 = (f32[1,224]{1,0:T(1,128)S(1)}, f32[1,224]{1,0:T(1,128)S(1)}, u32[]{:S(2)}, u32[]{:S(2)}) collective-permute-start(f32[1,224]{1,0:T(1,128)S(1)} %get-tuple-element.33), channel_id=1, source_target_pairs={{0,12},{1,13},{2,14},{3,15},{4,8},{5,9},{6,10},{7,11},{8,4},{9,5},... | collective-permute-start | bytes 2696 | tf_op jit(solution)/shard_map/ppermute | solution.py:34
  104.1 19.2 %collective-permute-start.13 = (f32[1,224]{1,0:T(1,128)S(1)}, f32[1,224]{1,0:T(1,128)S(1)}, u32[]{:S(2)}, u32[]{:S(2)}) collective-permute-start(f32[1,224]{1,0:T(1,128)S(1)} %get-tuple-element.32), channel_id=1, source_target_pairs={{0,13},{1,12},{2,15},{3,14},{4,9},{5,8},{6,11},{7,10},{8,5},{9,4},... | collective-permute-start | bytes 2696 | tf_op jit(solution)/shard_map/ppermute | solution.py:34
  106.0 17.3 %collective-permute-start.14 = (f32[1,224]{1,0:T(1,128)S(1)}, f32[1,224]{1,0:T(1,128)S(1)}, u32[]{:S(2)}, u32[]{:S(2)}) collective-permute-start(f32[1,224]{1,0:T(1,128)S(1)} %get-tuple-element.31), channel_id=1, source_target_pairs={{0,14},{1,15},{2,12},{3,13},{4,10},{5,11},{6,8},{7,9},{8,6},{9,7},... | collective-permute-start | bytes 2696 | tf_op jit(solution)/shard_map/ppermute | solution.py:34
  111.4 11.9 %collective-permute-start.15 = (f32[1,224]{1,0:T(1,128)S(1)}, f32[1,224]{1,0:T(1,128)S(1)}, u32[]{:S(2)}, u32[]{:S(2)}) collective-permute-start(f32[1,224]{1,0:T(1,128)S(1)} %get-tuple-element.30), channel_id=1, source_target_pairs={{0,15},{1,14},{2,13},{3,12},{4,11},{5,10},{6,9},{7,8},{8,7},{9,6},... | collective-permute-start | bytes 2696 | tf_op jit(solution)/shard_map/ppermute | solution.py:34
  115.6 7.8 %collective-permute-start.1 = (f32[1,224]{1,0:T(1,128)S(1)}, f32[1,224]{1,0:T(1,128)S(1)}, u32[]{:S(2)}, u32[]{:S(2)}) collective-permute-start(f32[1,224]{1,0:T(1,128)S(1)} %get-tuple-element.44), channel_id=1, source_target_pairs={{0,1},{1,0},{2,3},{3,2},{4,5},{5,4},{6,7},{7,6},{8,9},{9,8},{10,11... | collective-permute-start | bytes 2696 | tf_op jit(solution)/shard_map/ppermute | solution.py:34
  117.5 5.8 %collective-permute-start.2 = (f32[1,224]{1,0:T(1,128)S(1)}, f32[1,224]{1,0:T(1,128)S(1)}, u32[]{:S(2)}, u32[]{:S(2)}) collective-permute-start(f32[1,224]{1,0:T(1,128)S(1)} %get-tuple-element.43), channel_id=1, source_target_pairs={{0,2},{1,3},{2,0},{3,1},{4,6},{5,7},{6,4},{7,5},{8,10},{9,11},{10,... | collective-permute-start | bytes 2696 | tf_op jit(solution)/shard_map/ppermute | solution.py:34
  169.2 1.1 copy-start.4
  170.3 1.2 copy-start.2
  172.3 3.3 %collective-permute-start.16 = (f32[4,4,22,128]{3,1,0,2:T(4,128)S(1)}, f32[4,4,22,128]{3,1,0,2:T(4,128)S(1)}, u32[]{:S(2)}, u32[]{:S(2)}) collective-permute-start(f32[4,4,22,128]{3,1,0,2:T(4,128)S(1)} %copy.209), channel_id=1, source_target_pairs={{0,16},{16,0},{1,17},{17,1},{2,18},{18,2},{3,19},{19,3},{4,20},{20... | collective-permute-start | bytes 540680 | tf_op jit(solution)/shard_map/ppermute | solution.py:214
  176.9 17.4 %all-to-all-start.2 = ((f32[16,22,128]{2,1,0:T(8,128)}), f32[16,22,128]{2,1,0:T(8,128)S(1)}, u32[]{:S(2)}, u32[]{:S(2)}) async-start(f32[16,22,128]{2,1,0:T(8,128)} %copy.212), calls=%async_computation.2 | async-start | bytes 393216 | tf_op jit(solution)/shard_map/all_to_all | solution.py:239
  194.3 29.9 %copy-start.1 = (bf16[5120,160]{0,1:T(8,128)(2,1)S(1)}, bf16[5120,160]{0,1:T(8,128)(2,1)}, u32[]{:S(2)}) copy-start(bf16[5120,160]{0,1:T(8,128)(2,1)} %reshape.372) | copy-start | bytes 4915204
  196.2 27.8 %all-to-all-start.3 = ((bf16[32,20,128]{2,1,0:T(8,128)(2,1)}), bf16[32,20,128]{2,1,0:T(8,128)(2,1)S(1)}, u32[]{:S(2)}, u32[]{:S(2)}) async-start(bf16[32,20,128]{2,1,0:T(8,128)(2,1)} %broadcast_in_dim.112), calls=%async_computation.3 | async-start | bytes 393216 | tf_op jit(solution)/shard_map/all_to_all | solution.py:259
Sparse Core Ops, SparseCore 0:
  29.6 59.8 all-gather.3
